TPU v7x, 32 devices: a whole 2x2x4 slice. The times are simulated.
32 devices in a mesh: dp: 8 (over y, x, core), tensor: 4 (over z).
Axes of the slice: x: 2, y: 2, z: 4, core: 2. Of those that a mesh axis runs over, the one named last changes fastest.
Arguments:
- inputs: bfloat16 [16384, 768], P(('dp', 'tensor')), may hold values from -6 to 6
- cotangent: bfloat16 [16384, 768], P(('dp', 'tensor')), may hold values from -6 to 6
- lengths: int32 [128], P('dp'), may hold values from 25 to 128
- block_kind: int32 [32], P('dp'), may hold values from 0 to 1
- w_qkv: bfloat16 [2, 3, 768, 768], P(None, None, None, 'tensor'), may hold values from -0.3125 to 0.3125
- qv_bias: bfloat16 [2, 2, 768], P(None, None, 'tensor'), may hold values from -3 to 3
- w_out: bfloat16 [2, 768, 768], P(None, 'tensor'), may hold values from -0.625 to 0.625
- resid_bias: bfloat16 [2, 2, 768], replicated, may hold values from -3 to 3
- norm_gain: bfloat16 [2, 2, 768], replicated, may hold values from 0.5 to 1.5
- norm_shift: bfloat16 [2, 2, 768], replicated, may hold values from -2 to 2
- w_up: bfloat16 [2, 768, 3072], P(None, None, 'tensor'), may hold values from -0.21875 to 0.21875
- up_bias: bfloat16 [2, 3072], P(None, 'tensor'), may hold values from -3 to 3
- w_down: bfloat16 [2, 3072, 768], P(None, 'tensor'), may hold values from -0.15625 to 0.15625
Outputs:
- layer_out: bfloat16 [16384, 768], P(('dp', 'tensor'))
- input_grad: float32 [16384, 768], P(('dp', 'tensor'))
- grad_w_qkv: float32 [2, 3, 768, 768], P(None, None, None, 'tensor')
- grad_qv_bias: float32 [2, 2, 768], P(None, None, 'tensor')
- grad_w_out: float32 [2, 768, 768], P(None, 'tensor')
- grad_resid_bias: float32 [2, 2, 768], replicated
- grad_norm_gain: float32 [2, 2, 768], replicated
- grad_norm_shift: float32 [2, 2, 768], replicated
- grad_w_up: float32 [2, 768, 3072], P(None, None, 'tensor')
- grad_up_bias: float32 [2, 3072], P(None, 'tensor')
- grad_w_down: float32 [2, 3072, 768], P(None, 'tensor')
Inputs may be any that keep to these rules, and one draw needn't show every extreme that they name: lengths[s] is the number of real tokens of chain s; positions from lengths[s] on are padding and are never attended to. `block_kind`: block b holds chains b * 4 to (b+1) * 4 - 1, all heavy (0) or all light (1).
All inputs are finite; a program needn't handle non-finite values.
Results may differ from a plain program's by a relative error of at most 0.019.
The roundings to bfloat16 on the way count: a program that leaves them out, or rounds other values in their place, can miss the bound.
Values may be sent and summed in bfloat16 or wider, within the bound.
No kernel may reach another device: no remote copies, remote signals or barrier semaphores. Data moves between devices by JAX's collectives and lax.ppermute only.
A program may use at most 128 MiB of HBM per device.

v0:
```python
import jax
import jax.numpy as jnp
from jax import lax
from jax.sharding import PartitionSpec as P

HEAD_DIM = 64
CHAIN = 128
BLOCK_SEQS = 4
EPSILON = 1e-05
SQRT_HALF = 0.7071067811865476
INV_ROOT_TWO_PI = 0.3989422804014327


def norm_forward(row_data, gain_rows, shift_rows):
    mean_row = jnp.mean(row_data, axis=-1, keepdims=True)
    centred = row_data - mean_row
    var_row = jnp.mean(centred * centred, axis=-1, keepdims=True)
    inv_std = lax.rsqrt(var_row + EPSILON)
    unit_rows = centred * inv_std
    return (unit_rows * gain_rows + shift_rows, unit_rows, inv_std)


def norm_backward(grad_rows, gain_rows, unit_rows, inv_std):
    scaled = grad_rows * gain_rows
    mean_first = jnp.mean(scaled, axis=-1, keepdims=True)
    mean_second = jnp.mean(scaled * unit_rows, axis=-1, keepdims=True)
    return inv_std * (scaled - mean_first - unit_rows * mean_second)


def type_sum(kind_hot, values):
    return jnp.einsum("rt,rd->td", kind_hot, values, precision=lax.Precision.HIGHEST)


def gelu_slope(values):
    return 0.5 * (1.0 + lax.erf(values * SQRT_HALF)) + values * INV_ROOT_TWO_PI * jnp.exp(
        -0.5 * values * values
    )


def split_heads(row_data, heads_here):
    return row_data.reshape(BLOCK_SEQS, CHAIN, heads_here, HEAD_DIM)


def ffn_apply(up_w, ubias_w, down_w, row_blocks, kinds):

    def step(carry, packed):
        row_data, block_type = packed
        pre_act = jnp.dot(row_data, up_w[block_type], preferred_element_type=jnp.float32) + ubias_w[
            block_type
        ].astype(jnp.float32)
        activ = jax.nn.gelu(pre_act, approximate=False).astype(jnp.bfloat16)
        return (
            carry,
            (
                pre_act,
                activ,
                jnp.dot(activ, down_w[block_type], preferred_element_type=jnp.float32),
            ),
        )

    return lax.scan(step, 0, (row_blocks, kinds))[1]


def ffn_grad(up_w, ubias_w, down_w, row_blocks, grad_blocks, pre_blocks, activ_blocks, kinds):

    def step(accums, packed):
        acc_up, acc_ubias, acc_down = accums
        row_data, grad_rows, pre_act, activ, block_type = packed
        acc_down = acc_down.at[block_type].add(
            jnp.einsum("rf,rd->fd", activ, grad_rows, preferred_element_type=jnp.float32)
        )
        d_activ = jnp.einsum(
            "rd,fd->rf", grad_rows, down_w[block_type], preferred_element_type=jnp.float32
        ).astype(jnp.bfloat16)
        d_pre = (d_activ.astype(jnp.float32) * gelu_slope(pre_act)).astype(jnp.bfloat16)
        acc_up = acc_up.at[block_type].add(
            jnp.einsum("rd,rf->df", row_data, d_pre, preferred_element_type=jnp.float32)
        )
        acc_ubias = acc_ubias.at[block_type].add(jnp.sum(d_pre.astype(jnp.float32), axis=0))
        partial_back = jnp.einsum(
            "rf,df->rd", d_pre, up_w[block_type], preferred_element_type=jnp.float32
        )
        return ((acc_up, acc_ubias, acc_down), partial_back)

    zeros_ffn = (
        jnp.zeros(up_w.shape, jnp.float32),
        jnp.zeros(ubias_w.shape, jnp.float32),
        jnp.zeros(down_w.shape, jnp.float32),
    )
    return lax.scan(step, zeros_ffn, (row_blocks, grad_blocks, pre_blocks, activ_blocks, kinds))


def local(
    inputs,
    cotangent,
    lengths,
    block_kind,
    w_qkv,
    qv_bias,
    w_out,
    resid_bias,
    norm_gain,
    norm_shift,
    w_up,
    up_bias,
    w_down,
):
    tok_dev = inputs.shape[0]
    group_rows = tok_dev * lax.axis_size("tensor")
    block_rows = BLOCK_SEQS * CHAIN
    n_blocks = group_rows // block_rows
    heads_here = w_qkv.shape[3] // HEAD_DIM
    score_scale = HEAD_DIM ** (-0.5)
    highest = lax.Precision.HIGHEST
    row_block = (lax.axis_index("tensor") * tok_dev + jnp.arange(tok_dev)) // block_rows
    block_hot = row_block[:, None] == jnp.arange(n_blocks)[None, :]
    row_kind = jnp.sum(jnp.where(block_hot, block_kind[None, :], 0), axis=1)
    kind_hot = (row_kind[:, None] == jnp.arange(2)[None, :]).astype(jnp.float32)

    def pick(kind_table):
        return jnp.dot(kind_hot, kind_table.astype(jnp.float32), precision=highest)

    key_valid = jnp.arange(CHAIN)[None, :] < lengths[:, None]
    valid_blocks = key_valid.reshape(n_blocks, BLOCK_SEQS, CHAIN)

    def scores_of(query_rows, key_rows, valid_keys):
        raw_scores = (
            jnp.einsum(
                "sqhd,skhd->shqk",
                split_heads(query_rows, heads_here),
                split_heads(key_rows, heads_here),
                preferred_element_type=jnp.float32,
            )
            * score_scale
        )
        return jnp.where(valid_keys[:, None, None, :], raw_scores, -1e30)

    gathered = lax.all_gather(inputs, "tensor", axis=0, tiled=True)
    input_blocks = gathered.reshape(n_blocks, block_rows, -1)

    def attend_forward(accums, packed):
        row_data, valid_keys, block_type = packed
        projected = jnp.einsum(
            "rd,jde->jre", row_data, w_qkv[block_type], preferred_element_type=jnp.float32
        )
        bias_pair = qv_bias[block_type].astype(jnp.float32)
        query_rows = (projected[0] + bias_pair[0]).astype(jnp.bfloat16)
        key_rows = projected[1].astype(jnp.bfloat16)
        value_rows = (projected[2] + bias_pair[1]).astype(jnp.bfloat16)
        scores = scores_of(query_rows, key_rows, valid_keys)
        row_max = jnp.max(scores, axis=-1, keepdims=True)
        log_total = row_max[..., 0] + jnp.log(jnp.sum(jnp.exp(scores - row_max), axis=-1))
        attn_probs = jnp.exp(scores - log_total[..., None]).astype(jnp.bfloat16)
        mixed = jnp.einsum(
            "shqk,skhd->sqhd",
            attn_probs,
            split_heads(value_rows, heads_here),
            preferred_element_type=jnp.float32,
        )
        mixed = mixed.reshape(block_rows, -1).astype(jnp.bfloat16)
        partial_out = jnp.dot(mixed, w_out[block_type], preferred_element_type=jnp.float32)
        return (
            accums,
            (jnp.stack([query_rows, key_rows, value_rows]), log_total, mixed, partial_out),
        )

    unused, (kept_proj, kept_total, kept_mixed, attn_parts) = lax.scan(
        attend_forward, 0, (input_blocks, valid_blocks, block_kind)
    )
    attn_rows = lax.psum_scatter(
        attn_parts.reshape(group_rows, -1), "tensor", scatter_dimension=0, tiled=True
    )
    hidden_one = inputs.astype(jnp.float32) + attn_rows + pick(resid_bias[:, 0])
    gain_one = pick(norm_gain[:, 0])
    normed, unit_one, inv_one = norm_forward(hidden_one, gain_one, pick(norm_shift[:, 0]))
    normed_low = normed.astype(jnp.bfloat16)
    gathered_norm = lax.all_gather(normed_low, "tensor", axis=0, tiled=True)
    norm_blocks = gathered_norm.reshape(n_blocks, block_rows, -1)
    kept_pre, kept_activ, ffn_parts = ffn_apply(w_up, up_bias, w_down, norm_blocks, block_kind)
    ffn_rows = lax.psum_scatter(
        ffn_parts.reshape(group_rows, -1), "tensor", scatter_dimension=0, tiled=True
    )
    hidden_two = normed + ffn_rows + pick(resid_bias[:, 1])
    gain_two = pick(norm_gain[:, 1])
    output_rows, unit_two, inv_two = norm_forward(hidden_two, gain_two, pick(norm_shift[:, 1]))
    layer_out = output_rows.astype(jnp.bfloat16)
    grad_out = cotangent.astype(jnp.float32)
    d_two = norm_backward(grad_out, gain_two, unit_two, inv_two)
    d_two_low = d_two.astype(jnp.bfloat16)
    gathered_two = lax.all_gather(d_two_low, "tensor", axis=0, tiled=True)
    two_blocks = gathered_two.reshape(n_blocks, block_rows, -1)
    (acc_up, acc_ubias, acc_down), ffn_back_parts = ffn_grad(
        w_up, up_bias, w_down, norm_blocks, two_blocks, kept_pre, kept_activ, block_kind
    )
    d_normed = (
        lax.psum_scatter(
            ffn_back_parts.reshape(group_rows, -1), "tensor", scatter_dimension=0, tiled=True
        )
        + d_two
    )
    up_total, ubias_total, down_total = (acc_up, acc_ubias, acc_down)
    d_one = norm_backward(d_normed, gain_one, unit_one, inv_one)
    gain_grads = jnp.stack(
        [type_sum(kind_hot, d_normed * unit_one), type_sum(kind_hot, grad_out * unit_two)], axis=1
    )
    shift_grads = jnp.stack([type_sum(kind_hot, d_normed), type_sum(kind_hot, grad_out)], axis=1)
    rbias_grads = jnp.stack([type_sum(kind_hot, d_one), type_sum(kind_hot, d_two)], axis=1)
    gathered_one = lax.all_gather(d_one.astype(jnp.bfloat16), "tensor", axis=0, tiled=True)
    one_blocks = gathered_one.reshape(n_blocks, block_rows, -1)

    def attend_backward(accums, packed):
        acc_qkv, acc_qv, acc_out = accums
        row_data, grad_rows, valid_keys, kept_rows, log_total, mixed, block_type = packed
        acc_out = acc_out.at[block_type].add(
            jnp.einsum("re,rd->ed", mixed, grad_rows, preferred_element_type=jnp.float32)
        )
        d_mixed = jnp.einsum(
            "rd,ed->re", grad_rows, w_out[block_type], preferred_element_type=jnp.float32
        ).astype(jnp.bfloat16)
        scores = scores_of(kept_rows[0], kept_rows[1], valid_keys)
        attn_probs = jnp.exp(scores - log_total[..., None])
        d_mixed_heads = split_heads(d_mixed, heads_here)
        d_value = jnp.einsum(
            "shqk,sqhd->skhd",
            attn_probs.astype(jnp.bfloat16),
            d_mixed_heads,
            preferred_element_type=jnp.float32,
        )
        d_value = d_value.reshape(block_rows, -1).astype(jnp.bfloat16)
        d_probs = jnp.einsum(
            "sqhd,skhd->shqk",
            d_mixed_heads,
            split_heads(kept_rows[2], heads_here),
            preferred_element_type=jnp.float32,
        )
        prob_dot = jnp.sum(attn_probs * d_probs, axis=-1, keepdims=True)
        d_scores = (attn_probs * (d_probs - prob_dot)).astype(jnp.bfloat16)
        d_query = (
            jnp.einsum(
                "shqk,skhd->sqhd",
                d_scores,
                split_heads(kept_rows[1], heads_here),
                preferred_element_type=jnp.float32,
            )
            * score_scale
        )
        d_key = (
            jnp.einsum(
                "shqk,sqhd->skhd",
                d_scores,
                split_heads(kept_rows[0], heads_here),
                preferred_element_type=jnp.float32,
            )
            * score_scale
        )
        d_query = d_query.reshape(block_rows, -1).astype(jnp.bfloat16)
        d_key = d_key.reshape(block_rows, -1).astype(jnp.bfloat16)
        d_proj = jnp.stack([d_query, d_key, d_value])
        acc_qkv = acc_qkv.at[block_type].add(
            jnp.einsum("rd,jre->jde", row_data, d_proj, preferred_element_type=jnp.float32)
        )
        bias_sums = jnp.stack(
            [
                jnp.sum(d_query.astype(jnp.float32), axis=0),
                jnp.sum(d_value.astype(jnp.float32), axis=0),
            ]
        )
        acc_qv = acc_qv.at[block_type].add(bias_sums)
        partial_back = jnp.einsum(
            "jre,jde->rd", d_proj, w_qkv[block_type], preferred_element_type=jnp.float32
        )
        return ((acc_qkv, acc_qv, acc_out), partial_back)

    zeros_attn = (
        jnp.zeros(w_qkv.shape, jnp.float32),
        jnp.zeros(qv_bias.shape, jnp.float32),
        jnp.zeros(w_out.shape, jnp.float32),
    )
    (acc_qkv, acc_qv, acc_out), qkv_back_parts = lax.scan(
        attend_backward,
        zeros_attn,
        (input_blocks, one_blocks, valid_blocks, kept_proj, kept_total, kept_mixed, block_kind),
    )
    input_grad = (
        lax.psum_scatter(
            qkv_back_parts.reshape(group_rows, -1).astype(jnp.bfloat16),
            "tensor",
            scatter_dimension=0,
            tiled=True,
        ).astype(jnp.float32)
        + d_one
    )
    qkv_total, qv_total, out_total, up_total, ubias_total, down_total = lax.psum(
        (acc_qkv, acc_qv, acc_out, up_total, ubias_total, down_total), "dp"
    )
    rbias_total, gain_total, shift_total = lax.psum(
        (rbias_grads, gain_grads, shift_grads), ("dp", "tensor")
    )
    return (
        layer_out,
        input_grad,
        qkv_total,
        qv_total,
        out_total,
        rbias_total,
        gain_total,
        shift_total,
        up_total,
        ubias_total,
        down_total,
    )


def solution(mesh):
    return jax.shard_map(
        local,
        mesh=mesh,
        in_specs=(
            P(("dp", "tensor"), None),
            P(("dp", "tensor"), None),
            P("dp"),
            P("dp"),
            P(None, None, None, "tensor"),
            P(None, None, "tensor"),
            P(None, "tensor", None),
            P(),
            P(),
            P(),
            P(None, None, "tensor"),
            P(None, "tensor"),
            P(None, "tensor", None),
        ),
        out_specs=(
            P(("dp", "tensor"), None),
            P(("dp", "tensor"), None),
            P(None, None, None, "tensor"),
            P(None, None, "tensor"),
            P(None, "tensor", None),
            P(),
            P(),
            P(),
            P(None, None, "tensor"),
            P(None, "tensor"),
            P(None, "tensor", None),
        ),
        check_vma=False,
    )
```

profile of v0, /device:TPU:0, one launch (start us, length us, event | category | flops | bytes accessed | tf_op | source)
XLA Modules:
  0.0 1168.2 jit_solution(15813986910202748736)
XLA Ops:
  8.8 67.0 %all-gather.5.cloned.1.call-done = bf16[2048,768]{1,0:T(8,128)(2,1)} async-done(((bf16[512,768]{1,0:T(8,128)(2,1)}), bf16[2048,768]{1,0:T(8,128)(2,1)}) %all-gather.5.cloned.1.call-update) | async-done | bytes 3145744 | tf_op jit(solution)/shard_map/all_gather | solution.py:138
  75.8 3.2 broadcast.348.clone
  79.0 39.6 %while.68 = (s32[]{:T(128)}, bf16[4,3,512,192]{2,3,1,0:T(8,128)(2,1)}, f32[4,4,3,128]{3,2,1,0:T(4,128)S(1)}, bf16[4,512,192]{1,2,0:T(8,128)(2,1)S(1)}, f32[4,512...) while((s32[]{:T(128)}, ...), condition=%wide.region_3.4_spmd, body=%wide.region_0.3_spmd.sunk | while | flops 658340736 | bytes 15210975 | solution.py:167
  81.5 2.1 convolution_bitcast_fusion.7
  86.3 2.6 bitcast_dynamic-update-slice_fusion.15
  91.4 2.1 convolution_bitcast_fusion.7
  96.2 2.5 bitcast_dynamic-update-slice_fusion.15
  101.2 2.1 convolution_bitcast_fusion.7
  106.0 2.6 bitcast_dynamic-update-slice_fusion.15
  115.9 2.6 bitcast_dynamic-update-slice_fusion.15
  120.6 107.5 %reduce-scatter.5.cloned.1.call-done = f32[512,768]{1,0:T(8,128)} async-done(((f32[2048,768]{1,0:T(8,128)}), f32[512,768]{1,0:T(8,128)}) %reduce-scatter.5.cloned.1.call-update) | async-done | bytes 1572880 | tf_op jit(solution)/shard_map/reduce_scatter | solution.py:170
  228.1 2.1 fusion.155
  232.6 64.0 %all-gather.7.cloned.1.call-done = bf16[2048,768]{1,0:T(8,128)(2,1)} async-done(((bf16[512,768]{1,0:T(8,128)(2,1)}), bf16[2048,768]{1,0:T(8,128)(2,1)}) %all-gather.7.cloned.1.call-update) | async-done | bytes 3145744 | tf_op jit(solution)/shard_map/all_gather | solution.py:177
  296.6 3.2 broadcast.348.clone.1
  299.8 3.1 broadcast.348.clone.2
  303.0 48.6 %while.69 = (s32[]{:T(128)}, f32[4,512,768]{2,1,0:T(8,128)}, bf16[4,512,768]{2,1,0:T(8,128)(2,1)}, f32[4,512,768]{2,1,0:T(8,128)}, bf16[4,512,768]{2,1,0:T(8,128...) while((s32[]{:T(128)}, f32[4,512,768]{2,1,0:T(8,128)}, ...), condition=%wide.region_9.10_spmd, body=%wide.region_8.9_spmd.sunk | while | flops 1233912576 | bytes 21243096 | solution.py:61
  305.5 3.5 bitcast_dynamic-update-slice_fusion.16
  309.0 4.2 bitcast_dynamic-update-slice_fusion.17
  317.6 3.4 bitcast_dynamic-update-slice_fusion.16
  321.1 4.2 bitcast_dynamic-update-slice_fusion.17
  329.8 3.5 bitcast_dynamic-update-slice_fusion.16
  333.3 4.2 bitcast_dynamic-update-slice_fusion.17
  342.0 3.5 bitcast_dynamic-update-slice_fusion.16
  345.5 4.2 bitcast_dynamic-update-slice_fusion.17
  351.7 109.5 %reduce-scatter.7.cloned.1.call-done = f32[512,768]{1,0:T(8,128)} async-done(((f32[2048,768]{1,0:T(8,128)}), f32[512,768]{1,0:T(8,128)}) %reduce-scatter.7.cloned.1.call-update) | async-done | bytes 1572880 | tf_op jit(solution)/shard_map/reduce_scatter | solution.py:180
  461.2 2.4 fusion.157
  467.7 63.9 %all-gather.9.cloned.1.call-done = bf16[2048,768]{1,0:T(8,128)(2,1)} async-done(((bf16[512,768]{1,0:T(8,128)(2,1)}), bf16[2048,768]{1,0:T(8,128)(2,1)}) %all-gather.9.cloned.1.call-update) | async-done | bytes 3145744 | tf_op jit(solution)/shard_map/all_gather | solution.py:190
  531.5 2.5 broadcast.352
  534.0 2.5 broadcast.352.clone
  536.5 3.1 broadcast.348
  539.7 79.0 %while.70 = (s32[]{:T(128)}, f32[2,768,768]{2,1,0:T(8,128)}, f32[2,768]{1,0:T(2,128)S(1)}, f32[2,768,768]{2,1,0:T(8,128)}, f32[4,512,768]{2,1,0:T(8,128)}, /*ind...) while((s32[]{:T(128)}, f32[2,768,768]{2,1,0:T(8,128)}, ...), condition=%wide.region_19.20_spmd, body=%wide.region_15.19_spmd.sunk | while | flops 2423784192 | bytes 36199780 | solution.py:90
  542.2 3.1 convert_reduce_fusion.9
  546.1 4.7 fusion.226
  552.1 5.3 fusion.227
  561.9 3.1 convert_reduce_fusion.9
  565.8 4.7 fusion.226
  571.8 5.3 fusion.227
  577.1 2.1 bitcast_dynamic-update-slice_fusion.19
  581.7 3.1 convert_reduce_fusion.9
  585.6 4.7 fusion.226
  591.7 5.3 fusion.227
  601.4 3.1 convert_reduce_fusion.9
  605.3 4.7 fusion.226
  611.4 5.3 fusion.227
  619.2 109.0 %reduce-scatter.9.cloned.1.call-done = f32[512,768]{1,0:T(8,128)} async-done(((f32[2048,768]{1,0:T(8,128)}), f32[512,768]{1,0:T(8,128)}) %reduce-scatter.9.cloned.1.call-update) | async-done | bytes 1572880 | tf_op jit(solution)/shard_map/reduce_scatter | solution.py:196
  728.3 2.9 fusion.146
  735.0 62.2 %all-gather.11.cloned.1.call-done = bf16[2048,768]{1,0:T(8,128)(2,1)} async-done(((bf16[512,768]{1,0:T(8,128)(2,1)}), bf16[2048,768]{1,0:T(8,128)(2,1)}) %all-gather.11.cloned.1.call-update) | async-done | bytes 3145744 | tf_op jit(solution)/shard_map/all_gather | solution.py:208
  797.2 2.1 broadcast_in_dim.122
  800.4 95.7 %while.71 = (s32[]{:T(128)}, f32[2,3,768,192]{2,3,1,0:T(8,128)}, f32[2,2,192]{2,1,0:T(2,128)S(1)}, f32[2,192,768]{2,1,0:T(8,128)}, bf16[4,512,768]{2,1,0:T(8,128...) while((s32[]{:T(128)}, f32[2,3,768,192]{2,3,1,0:T(8,128)}, ...), condition=%wide.region_29.30_spmd, body=%wide.region_23.29_spmd.sunk | while | flops 1337720064 | bytes 39173132 | solution.py:279
  813.6 4.2 fusion.244
  819.4 3.2 fusion.245
  837.6 4.2 fusion.244
  843.3 3.2 fusion.245
  861.5 4.2 fusion.244
  867.2 3.2 fusion.245
  885.4 4.2 fusion.244
  891.2 3.2 fusion.245
  905.5 43.0 %all-reduce = (f32[2,2,768]{2,0,1:T(2,128)S(1)}, f32[2,2,768]{2,0,1:T(2,128)S(1)}, f32[2,2,768]{2,0,1:T(2,128)S(1)}) all-reduce(f32[2,2,768]{2,0,1:T(2,128)S(1)} %pad_maximum_fusion, f32[2,2,768]{2,0,1:T(2,128)S(1)} %pad_maximum_fusion.1, f32[2,2,768]{2,0,1:T(2,128)S(1)} %pad_maximum_fusion.2), channel_id=1, replica_groups=mesh['dp'=8,'tensor'=4] {'dp','tensor'}, use_global_device_ids=true, to_apply=%region_34.35 | all-reduce | flops 9216 | bytes 73728 | tf_op jit(solution)/shard_map/psum | solution.py:296
  950.3 24.0 %all-reduce.1 = (f32[2,2,192]{2,1,0:T(2,128)}, f32[2,768]{1,0:T(2,128)}) all-reduce(f32[2,2,192]{2,1,0:T(2,128)S(1)} %get-tuple-element.342, f32[2,768]{1,0:T(2,128)S(1)} %copy-done.25), channel_id=1, replica_groups=mesh['dp'=8,'tensor'=4] {'dp'}, use_global_device_ids=true, to_apply=%region_32.33 | all-reduce | flops 2304 | bytes 18432 | tf_op jit(solution)/shard_map/psum | solution.py:293
  974.3 2.4 convert_add_fusion
  976.7 173.9 %all-reduce.5.cloned.1.call-done = (f32[2,3,768,192]{2,3,1,0:T(8,128)}, f32[2,192,768]{2,1,0:T(8,128)}, f32[2,768,768]{2,1,0:T(8,128)}, f32[2,768,768]{2,1,0:T(8,128)}) async-done(((f32[2,3,768,192]{2,3,1,0:T(8,128)}, f32[2,192,768]{2,1,0:T(8,128)}, f32[2,768,768]{2,1,0:T(8,128)}, f32[2,768,768]{2,1,0:T(8,128)}), (f32[2,3,768,192]{2,3,1,0:T(8,128)}, f32[2,192,768]{2,1,0:T(8,128)}, f32[2,768,768]{2,1,0:T(8,128)}, ...) | async-done | bytes 14155792 | tf_op jit(solution)/shard_map/psum | solution.py:293
  1150.6 4.3 copy.275
  1156.0 2.4 copy.277
  1159.5 2.2 copy.278
  (511 shorter events, 128.3 us)
Async XLA Ops:
  7.2 68.6 %all-gather.5.cloned.1.call-start = ((), (), s32[]{:S(2)}) async-start(), calls=%async_computation.4 | async-start | bytes 3932160 | tf_op jit(solution)/shard_map/all_gather | solution.py:138
  7.9 220.2 %reduce-scatter.5.cloned.1.call-start = ((), (), s32[]{:S(2)}) async-start(), calls=%async_computation.5 | async-start | bytes 7864320 | tf_op jit(solution)/shard_map/reduce_scatter | solution.py:170
  75.8 3.2 copy-start.44
  75.8 3.2 copy-start.48
  119.5 177.2 %all-gather.7.cloned.1.call-start = ((), (), s32[]{:S(2)}) async-start(), calls=%async_computation.6 | async-start | bytes 3932160 | tf_op jit(solution)/shard_map/all_gather | solution.py:177
  120.6 109.9 %copy-start.17 = (f32[512,768]{1,0:T(8,128)}, f32[512,768]{1,0:T(8,128)S(1)}, u32[]{:S(2)}) copy-start(f32[512,768]{1,0:T(8,128)S(1)} %fusion.116) | copy-start | bytes 4718596
  230.2 501.0 %copy-start = (f32[512,768]{1,0:T(8,128)}, f32[512,768]{1,0:T(8,128)S(1)}, u32[]{:S(2)}) copy-start(f32[512,768]{1,0:T(8,128)S(1)} %get-tuple-element.566) | copy-start | bytes 4718596
  230.2 501.0 %copy-start.29 = (f32[512]{0:T(512)}, f32[512]{0:T(512)S(1)}, u32[]{:S(2)}) copy-start(f32[512]{0:T(512)S(1)} %broadcast_multiply_fusion.5) | copy-start | bytes 6148
  230.6 500.7 %copy-start.33 = (f32[512]{0:T(512)}, f32[512]{0:T(512)S(1)}, u32[]{:S(2)}) copy-start(f32[512]{0:T(512)S(1)} %add_rsqrt_fusion.1) | copy-start | bytes 6148
  232.5 228.7 %reduce-scatter.7.cloned.1.call-start = ((), (), s32[]{:S(2)}) async-start(), calls=%async_computation.7 | async-start | bytes 7864320 | tf_op jit(solution)/shard_map/reduce_scatter | solution.py:180
  299.8 3.1 copy-start.26
  309.0 4.2 copy-start.51
  321.1 4.2 copy-start.51
  333.3 4.2 copy-start.51
  345.5 4.2 copy-start.51
  351.6 179.9 %all-gather.9.cloned.1.call-start = ((), (), s32[]{:S(2)}) async-start(), calls=%async_computation.8 | async-start | bytes 3932160 | tf_op jit(solution)/shard_map/all_gather | solution.py:190
  467.5 260.8 %reduce-scatter.9.cloned.1.call-start = ((), (), s32[]{:S(2)}) async-start(), calls=%async_computation.9 | async-start | bytes 7864320 | tf_op jit(solution)/shard_map/reduce_scatter | solution.py:196
  536.5 3.1 copy-start.37
  536.5 3.1 copy-start.46
  545.3 5.5 copy-start.9
  552.1 5.3 copy-start.10
  552.1 5.3 copy-start.11
  565.0 5.5 copy-start.9
  571.8 5.3 copy-start.10
  571.8 5.3 copy-start.11
  584.8 5.5 copy-start.9
  591.6 5.3 copy-start.10
  591.6 5.3 copy-start.11
  604.5 5.5 copy-start.9
  611.4 5.3 copy-start.10
  611.4 5.3 copy-start.11
  619.2 177.9 %all-gather.11.cloned.1.call-start = ((), (), s32[]{:S(2)}) async-start(), calls=%async_computation.10 | async-start | bytes 3932160 | tf_op jit(solution)/shard_map/all_gather | solution.py:208
  733.1 241.2 %reduce-scatter.11.cloned.1.call-start = ((), (), s32[]{:S(2)}) async-start(), calls=%async_computation.11 | async-start | bytes 3932160 | tf_op jit(solution)/shard_map/reduce_scatter | solution.py:285
  800.4 3.8 copy-start.38
  800.4 5.4 copy-start.49
  800.4 5.8 copy-start.35
  805.8 3.3 copy-start.2
  813.6 4.4 copy-start.39
  818.0 4.5 copy-start.20
  824.3 3.8 copy-start.38
  824.3 5.5 copy-start.49
  824.3 5.8 copy-start.35
  829.7 3.3 copy-start.2
  837.6 4.4 copy-start.39
  841.9 4.5 copy-start.20
  848.2 3.8 copy-start.38
  848.2 5.5 copy-start.49
  848.2 5.8 copy-start.35
  853.6 3.3 copy-start.2
  861.5 4.4 copy-start.39
  865.8 4.5 copy-start.20
  872.1 3.8 copy-start.38
  872.1 5.5 copy-start.49
  872.1 5.8 copy-start.35
  877.6 3.3 copy-start.2
  885.4 4.4 copy-start.39
  889.8 4.5 copy-start.20
  896.0 254.5 %all-reduce.5.cloned.1.call-start = ((), (), s32[]{:S(2)}) async-start(), calls=%async_computation.12 | async-start | bytes 28311552 | tf_op jit(solution)/shard_map/psum | solution.py:293
  904.6 45.6 %copy-start.25 = (f32[2,768]{1,0:T(2,128)S(1)}, f32[2,768]{1,0:T(2,128)}, u32[]{:S(2)}) copy-start(f32[2,768]{1,0:T(2,128)} %copy-done.24) | copy-start | bytes 18436
  904.7 69.6 %copy-start.15 = (f32[512,768]{1,0:T(8,128)S(1)}, f32[512,768]{1,0:T(8,128)}, u32[]{:S(2)}) copy-start(f32[512,768]{1,0:T(8,128)} %get-tuple-element.534) | copy-start | bytes 4718596
  1150.6 4.4 copy-start.23
  1150.6 5.4 copy-start.21
  1155.0 4.2 slice-start
  1156.0 3.6 slice-start.1
  (53 other events, 88.7 us)
Sparse Core Ops, SparseCore 0:
  9.6 66.1 all-gather.4
  118.7 109.3 reduce-scatter.4
  232.6 63.9 all-gather.6
  351.7 109.4 reduce-scatter.6
  467.6 63.9 all-gather.8
  618.8 109.4 reduce-scatter.8
  733.2 63.9 all-gather.10
  896.2 59.9 reduce-scatter.10
  961.4 189.1 all-reduce.4
where the time goes:
time: 1170 us
  waiting for transfers between devices  758 us (65%)
  matrix products  172 us (15%)
  local copies, waits for them, and re-layouts  73.4 us (6%)
  blocking collectives  67 us (6%)
  other arithmetic  50 us (4%)
  loops' own time  32.5 us (3%)
  between operations  14.2 us (1%)
    psum x1, waiting for transfers between devices, local(): lax.psum((acc_qkv, acc_qv, acc_out, up_total, ubias_total, down_total), '...  174 us
    reduce_scatter x1, waiting for transfers between devices, local(): lax.psum_scatter(ffn_parts.reshape(group_rows, -1), 'tensor', scatter_dim...  110 us
    reduce_scatter x1, waiting for transfers between devices, local(): lax.psum_scatter(ffn_back_parts.reshape(group_rows, -1), 'tensor', scatte...  109 us
    reduce_scatter x1, waiting for transfers between devices, local(): lax.psum_scatter(attn_parts.reshape(group_rows, -1), 'tensor', scatter_di...  107 us
    all_gather x1, waiting for transfers between devices, local(): gathered = lax.all_gather(inputs, 'tensor', axis=0, tiled=True)  67 us
    all_gather x1, waiting for transfers between devices, local(): gathered_norm = lax.all_gather(normed_low, 'tensor', axis=0, tiled=True)  64 us
    all_gather x1, waiting for transfers between devices, local(): gathered_two = lax.all_gather(d_two_low, 'tensor', axis=0, tiled=True)  63.9 us
    all_gather x1, waiting for transfers between devices, local(): lax.all_gather(d_one.astype(jnp.bfloat16), 'tensor', axis=0, tiled=True)  62.2 us
  transfers between devices with their start and end apart: 9, of which 8 were waited for; matrix products, arithmetic and copies ran while one was open for 1% of the time, Pallas kernels for 0%

commit v1 on v0

--- a/solution.py
+++ b/solution.py
@@ -9,6 +9,27 @@
 EPSILON = 1e-05
 SQRT_HALF = 0.7071067811865476
 INV_ROOT_TWO_PI = 0.3989422804014327
+
+
+def joined_along(pieces, dim):
+    pieces = jnp.moveaxis(pieces, 0, dim)
+    shape = pieces.shape
+    return pieces.reshape(*shape[:dim], shape[dim] * shape[dim + 1], *shape[dim + 2 :])
+
+
+def doubled(x, axis):
+    size, index = (lax.axis_size(axis), lax.axis_index(axis))
+    blocks, distance = (x[None], 1)
+    while distance < size:
+        other = lax.ppermute(blocks, axis, [(i, i ^ distance) for i in range(size)])
+        low = index & distance == 0
+        blocks = jnp.concatenate([jnp.where(low, blocks, other), jnp.where(low, other, blocks)])
+        distance *= 2
+    return blocks
+
+
+def collect(value, axis, dim):
+    return joined_along(doubled(value, axis), dim)
 
 
 def norm_forward(row_data, gain_rows, shift_rows):
@@ -205,7 +226,7 @@
     )
     shift_grads = jnp.stack([type_sum(kind_hot, d_normed), type_sum(kind_hot, grad_out)], axis=1)
     rbias_grads = jnp.stack([type_sum(kind_hot, d_one), type_sum(kind_hot, d_two)], axis=1)
-    gathered_one = lax.all_gather(d_one.astype(jnp.bfloat16), "tensor", axis=0, tiled=True)
+    gathered_one = collect(d_one.astype(jnp.bfloat16), "tensor", 0)
     one_blocks = gathered_one.reshape(n_blocks, block_rows, -1)
 
     def attend_backward(accums, packed):

time: 1170 us -> 1210 us (1.034)
  waiting for transfers between devices: 758 us -> 781 us
    ppermute x0 -> x2, waiting for transfers between devices: none -> 83.7 us  [doubled(): other = lax.ppermute(blocks, axis, [(i, i ^ distance) for i in range(size)])]
    all_gather x1 -> x0, waiting for transfers between devices: 62.2 us -> none  [local(): lax.all_gather(d_one.astype(jnp.bfloat16), 'tensor', axis=0, tiled=True)]
  transfers between devices with their start and end apart: 9 -> 10, of which waited for: 8 -> 9; matrix products, arithmetic and copies ran while one was open for 1% -> 1% of each run, Pallas kernels for 0% -> 0%
where the time goes in v1:
time: 1210 us
  waiting for transfers between devices  781 us (65%)
  matrix products  171 us (14%)
  local copies, waits for them, and re-layouts  78.7 us (7%)
  blocking collectives  67.8 us (6%)
  other arithmetic  59.5 us (5%)
  loops' own time  31.9 us (3%)
  between operations  14.5 us (1%)
    psum x1, waiting for transfers between devices, local(): lax.psum((acc_qkv, acc_qv, acc_out, up_total, ubias_total, down_total), '...  174 us
    reduce_scatter x1, waiting for transfers between devices, local(): lax.psum_scatter(ffn_parts.reshape(group_rows, -1), 'tensor', scatter_dim...  110 us
    reduce_scatter x1, waiting for transfers between devices, local(): lax.psum_scatter(ffn_back_parts.reshape(group_rows, -1), 'tensor', scatte...  109 us
    reduce_scatter x1, waiting for transfers between devices, local(): lax.psum_scatter(attn_parts.reshape(group_rows, -1), 'tensor', scatter_di...  108 us
    ppermute x2, waiting for transfers between devices, doubled(): other = lax.ppermute(blocks, axis, [(i, i ^ distance) for i in range(size)])  83.7 us
    all_gather x1, waiting for transfers between devices, local(): gathered = lax.all_gather(inputs, 'tensor', axis=0, tiled=True)  67 us
    all_gather x1, waiting for transfers between devices, local(): gathered_norm = lax.all_gather(normed_low, 'tensor', axis=0, tiled=True)  64 us
    all_gather x1, waiting for transfers between devices, local(): gathered_two = lax.all_gather(d_two_low, 'tensor', axis=0, tiled=True)  63.9 us
  transfers between devices with their start and end apart: 10, of which 9 were waited for; matrix products, arithmetic and copies ran while one was open for 1% of the time, Pallas kernels for 0%

profile of v1, /device:TPU:0, one launch (start us, length us, event | category | flops | bytes accessed | tf_op | source)
XLA Modules:
  0.0 1208.9 jit_solution(10340863823736230984)
XLA Ops:
  8.8 67.0 %all-gather.4.cloned.1.call-done = bf16[2048,768]{1,0:T(8,128)(2,1)} async-done(((bf16[512,768]{1,0:T(8,128)(2,1)}), bf16[2048,768]{1,0:T(8,128)(2,1)}) %all-gather.4.cloned.1.call-update) | async-done | bytes 3145744 | tf_op jit(solution)/shard_map/all_gather | solution.py:159
  75.8 3.2 broadcast.350.clone
  79.0 43.5 %while.68 = (s32[]{:T(128)}, bf16[4,3,512,192]{2,3,1,0:T(8,128)(2,1)}, f32[4,4,3,128]{3,2,1,0:T(4,128)}, bf16[4,512,192]{1,2,0:T(8,128)(2,1)}, f32[4,512,768]{2,...) while((s32[]{:T(128)}, ...), condition=%wide.region_3.4_spmd, body=%wide.region_0.3_spmd.sunk | while | flops 658340736 | bytes 15204931 | solution.py:188
  87.3 2.6 bitcast_dynamic-update-slice_fusion.15
  98.2 2.5 bitcast_dynamic-update-slice_fusion.15
  109.0 2.6 bitcast_dynamic-update-slice_fusion.15
  119.9 2.6 bitcast_dynamic-update-slice_fusion.15
  124.3 107.8 %reduce-scatter.5.cloned.1.call-done = f32[512,768]{1,0:T(8,128)} async-done(((f32[2048,768]{1,0:T(8,128)}), f32[512,768]{1,0:T(8,128)}) %reduce-scatter.5.cloned.1.call-update) | async-done | bytes 1572880 | tf_op jit(solution)/shard_map/reduce_scatter | solution.py:191
  232.1 2.1 fusion.154
  236.5 64.0 %all-gather.6.cloned.1.call-done = bf16[2048,768]{1,0:T(8,128)(2,1)} async-done(((bf16[512,768]{1,0:T(8,128)(2,1)}), bf16[2048,768]{1,0:T(8,128)(2,1)}) %all-gather.6.cloned.1.call-update) | async-done | bytes 3145744 | tf_op jit(solution)/shard_map/all_gather | solution.py:198
  300.6 3.2 broadcast.350.clone.1
  303.8 3.1 broadcast.350.clone.2
  306.9 48.7 %while.69 = (s32[]{:T(128)}, f32[4,512,768]{2,1,0:T(8,128)}, bf16[4,512,768]{2,1,0:T(8,128)(2,1)}, f32[4,512,768]{2,1,0:T(8,128)}, bf16[4,512,768]{2,1,0:T(8,128...) while((s32[]{:T(128)}, f32[4,512,768]{2,1,0:T(8,128)}, ...), condition=%wide.region_9.10_spmd, body=%wide.region_8.9_spmd.sunk | while | flops 1233912576 | bytes 21243096 | solution.py:82
  309.5 3.5 bitcast_dynamic-update-slice_fusion.16
  313.0 4.2 bitcast_dynamic-update-slice_fusion.17
  321.6 3.4 bitcast_dynamic-update-slice_fusion.16
  325.1 4.2 bitcast_dynamic-update-slice_fusion.17
  329.2 2.1 bitcast_dynamic-update-slice_fusion.18
  333.8 3.5 bitcast_dynamic-update-slice_fusion.16
  337.3 4.2 bitcast_dynamic-update-slice_fusion.17
  346.0 3.5 bitcast_dynamic-update-slice_fusion.16
  349.5 4.2 bitcast_dynamic-update-slice_fusion.17
  355.7 109.5 %reduce-scatter.7.cloned.1.call-done = f32[512,768]{1,0:T(8,128)} async-done(((f32[2048,768]{1,0:T(8,128)}), f32[512,768]{1,0:T(8,128)}) %reduce-scatter.7.cloned.1.call-update) | async-done | bytes 1572880 | tf_op jit(solution)/shard_map/reduce_scatter | solution.py:201
  465.2 2.4 fusion.156
  471.7 63.9 %all-gather.8.cloned.1.call-done = bf16[2048,768]{1,0:T(8,128)(2,1)} async-done(((bf16[512,768]{1,0:T(8,128)(2,1)}), bf16[2048,768]{1,0:T(8,128)(2,1)}) %all-gather.8.cloned.1.call-update) | async-done | bytes 3145744 | tf_op jit(solution)/shard_map/all_gather | solution.py:211
  535.6 2.5 broadcast.355
  538.1 2.5 broadcast.355.clone
  540.6 3.1 broadcast.350
  543.7 80.4 %while.70 = (s32[]{:T(128)}, f32[2,768,768]{2,1,0:T(8,128)}, f32[2,768]{1,0:T(2,128)S(1)}, f32[2,768,768]{2,1,0:T(8,128)}, f32[4,512,768]{2,1,0:T(8,128)}, /*ind...) while((s32[]{:T(128)}, f32[2,768,768]{2,1,0:T(8,128)}, ...), condition=%wide.region_19.20_spmd, body=%wide.region_15.19_spmd.sunk | while | flops 2423784192 | bytes 36199780 | solution.py:111
  546.2 3.1 convert_reduce_fusion.9
  550.2 4.8 fusion.225
  556.5 5.3 fusion.226
  566.3 3.1 convert_reduce_fusion.9
  570.2 4.8 fusion.225
  576.6 5.3 fusion.226
  581.8 2.1 bitcast_dynamic-update-slice_fusion.19
  586.5 3.1 convert_reduce_fusion.9
  590.4 4.8 fusion.225
  596.7 5.3 fusion.226
  606.5 3.1 convert_reduce_fusion.9
  610.5 4.8 fusion.225
  616.8 5.3 fusion.226
  624.7 109.0 %reduce-scatter.9.cloned.1.call-done = f32[512,768]{1,0:T(8,128)} async-done(((f32[2048,768]{1,0:T(8,128)}), f32[512,768]{1,0:T(8,128)}) %reduce-scatter.9.cloned.1.call-update) | async-done | bytes 1572880 | tf_op jit(solution)/shard_map/reduce_scatter | solution.py:217
  733.7 2.9 fusion.146
  740.0 18.1 %collective-permute-done = bf16[1,512,768]{2,1,0:T(8,128)(2,1)} collective-permute-done((bf16[1,512,768]{2,1,0:T(8,128)(2,1)}, bf16[1,512,768]{2,1,0:T(8,128)(2,1)}, u32[]{:S(2)}, u32[]{:S(2)}) %collective-permute-start) | collective-permute-done | bytes 786464 | tf_op jit(solution)/shard_map/ppermute | solution.py:24
  760.8 2.9 collective-permute-start.1
  765.5 65.7 %collective-permute-done.1 = bf16[2,512,768]{2,1,0:T(8,128)(2,1)} collective-permute-done((bf16[2,512,768]{2,1,0:T(8,128)(2,1)}, bf16[2,512,768]{2,1,0:T(8,128)(2,1)}, u32[]{:S(2)}, u32[]{:S(2)}) %collective-permute-start.1) | collective-permute-done | bytes 1572896 | tf_op jit(solution)/shard_map/ppermute | solution.py:24
  834.7 2.1 broadcast_in_dim.125
  837.9 97.0 %while.71 = (s32[]{:T(128)}, f32[2,3,768,192]{2,3,1,0:T(8,128)}, f32[2,2,192]{2,1,0:T(2,128)S(1)}, f32[2,192,768]{2,1,0:T(8,128)}, bf16[4,512,768]{2,1,0:T(8,128...) while((s32[]{:T(128)}, f32[2,3,768,192]{2,3,1,0:T(8,128)}, ...), condition=%wide.region_29.30_spmd, body=%wide.region_23.29_spmd.sunk | while | flops 1337720064 | bytes 38976468 | solution.py:300
  851.8 4.2 fusion.243
  857.4 3.1 fusion.244
  876.0 4.2 fusion.243
  881.6 3.1 fusion.244
  900.3 4.2 fusion.243
  905.9 3.1 fusion.244
  924.6 4.2 fusion.243
  930.2 3.1 fusion.244
  944.6 43.8 %all-reduce = (f32[2,2,768]{2,0,1:T(2,128)S(1)}, f32[2,2,768]{2,0,1:T(2,128)S(1)}, f32[2,2,768]{2,0,1:T(2,128)S(1)}) all-reduce(f32[2,2,768]{2,0,1:T(2,128)S(1)} %pad_maximum_fusion.2, f32[2,2,768]{2,0,1:T(2,128)S(1)} %pad_maximum_fusion.3, f32[2,2,768]{2,0,1:T(2,128)S(1)} %pad_maximum_fusion.4), channel_id=1, replica_groups=mesh['dp'=8,'tensor'=4] {'dp','tensor'}, use_global_device_ids=true, to_apply=%region_34.35 | all-reduce | flops 9216 | bytes 73728 | tf_op jit(solution)/shard_map/psum | solution.py:317
  990.2 24.0 %all-reduce.1 = (f32[2,2,192]{2,1,0:T(2,128)}, f32[2,768]{1,0:T(2,128)}) all-reduce(f32[2,2,192]{2,1,0:T(2,128)S(1)} %get-tuple-element.342, f32[2,768]{1,0:T(2,128)S(1)} %copy-done.25), channel_id=1, replica_groups=mesh['dp'=8,'tensor'=4] {'dp'}, use_global_device_ids=true, to_apply=%region_32.33 | all-reduce | flops 2304 | bytes 18432 | tf_op jit(solution)/shard_map/psum | solution.py:314
  1014.2 2.4 convert_add_fusion
  1016.6 174.4 %all-reduce.5.cloned.1.call-done = (f32[2,3,768,192]{2,3,1,0:T(8,128)}, f32[2,192,768]{2,1,0:T(8,128)}, f32[2,768,768]{2,1,0:T(8,128)}, f32[2,768,768]{2,1,0:T(8,128)}) async-done(((f32[2,3,768,192]{2,3,1,0:T(8,128)}, f32[2,192,768]{2,1,0:T(8,128)}, f32[2,768,768]{2,1,0:T(8,128)}, f32[2,768,768]{2,1,0:T(8,128)}), (f32[2,3,768,192]{2,3,1,0:T(8,128)}, f32[2,192,768]{2,1,0:T(8,128)}, f32[2,768,768]{2,1,0:T(8,128)}, ...) | async-done | bytes 14155792 | tf_op jit(solution)/shard_map/psum | solution.py:314
  1191.0 4.3 copy.275
  1196.4 2.4 copy.277
  1199.9 2.2 copy.278
  (508 shorter events, 147.6 us)
Async XLA Ops:
  7.2 68.6 %all-gather.4.cloned.1.call-start = ((), (), s32[]{:S(2)}) async-start(), calls=%async_computation.4 | async-start | bytes 3932160 | tf_op jit(solution)/shard_map/all_gather | solution.py:159
  7.9 224.2 %reduce-scatter.5.cloned.1.call-start = ((), (), s32[]{:S(2)}) async-start(), calls=%async_computation.5 | async-start | bytes 7864320 | tf_op jit(solution)/shard_map/reduce_scatter | solution.py:191
  75.8 3.2 copy-start.20
  75.8 3.2 copy-start.42
  75.8 3.2 copy-start.46
  86.3 3.5 copy-start.47
  97.2 3.5 copy-start.47
  108.1 3.5 copy-start.47
  118.9 3.5 copy-start.47
  123.1 177.5 %all-gather.6.cloned.1.call-start = ((), (), s32[]{:S(2)}) async-start(), calls=%async_computation.6 | async-start | bytes 3932160 | tf_op jit(solution)/shard_map/all_gather | solution.py:198
  124.3 110.3 %copy-start.17 = (f32[512,768]{1,0:T(8,128)}, f32[512,768]{1,0:T(8,128)S(1)}, u32[]{:S(2)}) copy-start(f32[512,768]{1,0:T(8,128)S(1)} %fusion.116) | copy-start | bytes 4718596
  234.2 502.4 %copy-start = (f32[512,768]{1,0:T(8,128)}, f32[512,768]{1,0:T(8,128)S(1)}, u32[]{:S(2)}) copy-start(f32[512,768]{1,0:T(8,128)S(1)} %get-tuple-element.570) | copy-start | bytes 4718596
  234.2 502.4 %copy-start.29 = (f32[512]{0:T(512)}, f32[512]{0:T(512)S(1)}, u32[]{:S(2)}) copy-start(f32[512]{0:T(512)S(1)} %broadcast_multiply_fusion.5) | copy-start | bytes 6148
  234.5 502.1 %copy-start.33 = (f32[512]{0:T(512)}, f32[512]{0:T(512)S(1)}, u32[]{:S(2)}) copy-start(f32[512]{0:T(512)S(1)} %add_rsqrt_fusion.1) | copy-start | bytes 6148
  236.5 228.7 %reduce-scatter.7.cloned.1.call-start = ((), (), s32[]{:S(2)}) async-start(), calls=%async_computation.7 | async-start | bytes 7864320 | tf_op jit(solution)/shard_map/reduce_scatter | solution.py:201
  313.0 4.2 copy-start.50
  325.1 4.2 copy-start.50
  337.3 4.2 copy-start.50
  349.5 4.2 copy-start.50
  355.6 179.9 %all-gather.8.cloned.1.call-start = ((), (), s32[]{:S(2)}) async-start(), calls=%async_computation.8 | async-start | bytes 3932160 | tf_op jit(solution)/shard_map/all_gather | solution.py:211
  471.5 262.2 %reduce-scatter.9.cloned.1.call-start = ((), (), s32[]{:S(2)}) async-start(), calls=%async_computation.9 | async-start | bytes 7864320 | tf_op jit(solution)/shard_map/reduce_scatter | solution.py:217
  540.5 3.1 copy-start.44
  549.3 5.6 copy-start.9
  556.5 5.3 copy-start.10
  556.5 5.3 copy-start.11
  569.4 5.6 copy-start.9
  576.5 5.3 copy-start.10
  576.5 5.3 copy-start.11
  589.6 5.6 copy-start.9
  596.7 5.3 copy-start.10
  596.7 5.3 copy-start.11
  609.6 5.6 copy-start.9
  616.8 5.3 copy-start.10
  616.8 5.3 copy-start.11
  624.7 389.5 %reduce-scatter.11.cloned.1.call-start = ((), (), s32[]{:S(2)}) async-start(), calls=%async_computation.10 | async-start | bytes 3932160 | tf_op jit(solution)/shard_map/reduce_scatter | solution.py:306
  738.5 19.5 %collective-permute-start = (bf16[1,512,768]{2,1,0:T(8,128)(2,1)}, bf16[1,512,768]{2,1,0:T(8,128)(2,1)}, u32[]{:S(2)}, u32[]{:S(2)}) collective-permute-start(bf16[1,512,768]{2,1,0:T(8,128)(2,1)} %get-tuple-element.533), channel_id=1, source_target_pairs={{0,1},{1,0},{2,3},{3,2},{4,5},{5,4},{6,7},{7,6},{8,9},{9,8},{10,11... | collective-permute-start | bytes 2359304 | tf_op jit(solution)/shard_map/ppermute | solution.py:24
  760.8 70.4 %collective-permute-start.1 = (bf16[2,512,768]{2,1,0:T(8,128)(2,1)}, bf16[2,512,768]{2,1,0:T(8,128)(2,1)}, u32[]{:S(2)}, u32[]{:S(2)}) collective-permute-start(bf16[2,512,768]{2,1,0:T(8,128)(2,1)} %pad_maximum_fusion.1), channel_id=1, source_target_pairs={{0,2},{1,3},{2,0},{3,1},{4,6},{5,7},{6,4},{7,5},{8,10},{9,11},{10,... | collective-permute-start | bytes 4718600 | tf_op jit(solution)/shard_map/ppermute | solution.py:24
  837.9 3.7 copy-start.36
  837.9 5.3 copy-start.48
  843.3 3.9 copy-start.2
  851.8 4.3 copy-start.37
  856.1 4.4 copy-start.21
  862.2 3.7 copy-start.36
  862.2 5.3 copy-start.48
  867.5 3.9 copy-start.2
  876.0 4.3 copy-start.37
  880.4 4.4 copy-start.21
  886.4 3.7 copy-start.36
  886.4 5.3 copy-start.48
  891.8 3.9 copy-start.2
  900.3 4.3 copy-start.37
  904.6 4.4 copy-start.21
  910.7 3.7 copy-start.36
  910.7 5.3 copy-start.48
  916.1 3.9 copy-start.2
  924.6 4.3 copy-start.37
  928.9 4.4 copy-start.21
  935.0 256.0 %all-reduce.5.cloned.1.call-start = ((), (), s32[]{:S(2)}) async-start(), calls=%async_computation.11 | async-start | bytes 28311552 | tf_op jit(solution)/shard_map/psum | solution.py:314
  943.8 46.4 %copy-start.25 = (f32[2,768]{1,0:T(2,128)S(1)}, f32[2,768]{1,0:T(2,128)}, u32[]{:S(2)}) copy-start(f32[2,768]{1,0:T(2,128)} %copy-done.24) | copy-start | bytes 18436
  943.8 70.4 %copy-start.15 = (f32[512,768]{1,0:T(8,128)S(1)}, f32[512,768]{1,0:T(8,128)}, u32[]{:S(2)}) copy-start(f32[512,768]{1,0:T(8,128)} %get-tuple-element.534) | copy-start | bytes 4718596
  1191.0 4.4 copy-start.23
  1191.0 5.4 copy-start.22
  1195.4 4.2 slice-start
  1196.4 3.6 slice-start.1
  (50 other events, 85.4 us)
Sparse Core Ops, SparseCore 0:
  9.6 66.1 all-gather.3
  122.7 109.3 reduce-scatter.4
  236.6 63.9 all-gather.5
  355.7 109.4 reduce-scatter.6
  471.6 63.9 all-gather.7
  624.2 109.4 reduce-scatter.8
  935.1 61.4 reduce-scatter.10
  1001.8 189.1 all-reduce.4
